TPU v7x, 32 devices: a whole 2x2x4 slice. The times are simulated.
32 devices in a mesh: freq: 4 (over y, core), row: 8 (over z, x).
Axes of the slice: x: 2, y: 2, z: 4, core: 2. Of those that a mesh axis runs over, the one named last changes fastest.
Arguments:
- traces: bfloat16 [2, 8192, 8192], P(None, ('freq', 'row')), may hold values from -1.1953125 to 1.1953125
- prior: bfloat16 [4, 2, 8192, 8192], P('freq', None, None, 'row'), may hold values from -0.796875 to 0.796875
- bins: int32 [4], replicated, may hold values from 64 to 255
- panels: int32 [2], replicated, may hold values from 0 to 31
Outputs:
- multiples: bfloat16 [4, 2, 8192, 8192], P('freq', None, 'row')
- spectrum: bfloat16 [4, 2, 8192, 8192], P('freq', None, None, 'row')
All inputs are finite; a program needn't handle non-finite values.
Results may differ from a plain program's by a relative error of at most 0.0077.
Values may be sent and summed in bfloat16 or wider, within the bound.
No kernel may reach another device: no remote copies, remote signals or barrier semaphores. Data moves between devices by JAX's collectives and lax.ppermute only.
A program may use at most 640 MiB of HBM per device.

v0:
```python
import math
import jax
import jax.numpy as jnp
from jax import lax
from jax.sharding import PartitionSpec as P

NT_REC = 1024
PANEL = 256
STEPS = 2
BLOCK_START = 1022


def spread(value, axis, source):
    kept = jnp.where(lax.axis_index(axis) == source, value, 0).astype(value.dtype)
    return lax.psum(kept, axis)


def complex_terms(left, right):
    dims = (((0,), (1,)), ((), ()))

    def product(first, second):
        return lax.dot_general(first, second, dims, preferred_element_type=jnp.float32)

    real_part = product(left[0], right[0]) - product(left[1], right[1])
    imag_part = product(left[0], right[1]) + product(left[1], right[0])
    return (real_part, imag_part)


def body(traces, prior, bins, panels):
    sample_count, shots_local, receivers = traces.shape
    row_count = lax.axis_size("row")
    freq_count = lax.axis_size("freq")
    block_rows = receivers // row_count
    sample_index = BLOCK_START + jnp.arange(sample_count, dtype=jnp.int32)
    turn_count = bins[:, None] * sample_index[None, :] % NT_REC
    angles = 2.0 * math.pi / NT_REC * turn_count.astype(jnp.float32)
    twiddle = jnp.stack([jnp.cos(angles), -jnp.sin(angles)], axis=1).astype(jnp.bfloat16)
    blocked = traces.reshape(sample_count, shots_local, row_count, block_rows)
    transformed = jnp.einsum(
        "tsqb,fct->fqcsb", blocked, twiddle, preferred_element_type=jnp.float32
    ).astype(jnp.bfloat16)
    grouped = transformed.reshape(freq_count * row_count, 2, shots_local, block_rows)
    arrived = lax.all_to_all(grouped, ("freq", "row"), split_axis=0, concat_axis=2, tiled=True)
    arrived = arrived.reshape(2, freq_count * row_count * shots_local, block_rows)
    spectrum = (prior[0].astype(jnp.float32) + arrived.astype(jnp.float32)).astype(jnp.bfloat16)
    panels_each = block_rows // PANEL
    real_sum = jnp.zeros((block_rows, receivers), jnp.float32)
    imag_sum = jnp.zeros((block_rows, receivers), jnp.float32)
    for panel_step in range(STEPS):
        chosen = panels[panel_step]
        owner = chosen // panels_each
        offset = chosen % panels_each * PANEL
        own_rows = lax.dynamic_slice_in_dim(spectrum, offset, PANEL, 2)
        panel_data = spread(own_rows, "row", owner)
        left = lax.dynamic_slice_in_dim(spectrum, chosen * PANEL, PANEL, 1)
        real_part, imag_part = complex_terms(left, panel_data)
        real_sum = real_sum + real_part
        imag_sum = imag_sum + imag_part
    return (jnp.stack([real_sum, imag_sum])[None].astype(jnp.bfloat16), spectrum[None])


def solution(mesh):
    return jax.shard_map(
        body,
        mesh=mesh,
        in_specs=(P(None, ("freq", "row"), None), P("freq", None, None, "row"), P(), P()),
        out_specs=(P("freq", None, "row", None), P("freq", None, None, "row")),
        check_vma=False,
    )
```

profile of v0, /device:TPU:0, one launch (start us, length us, event | category | flops | bytes accessed | tf_op | source)
XLA Modules:
  0.0 1675.5 jit_solution(10062186824207716788)
XLA Ops:
  7.2 16.5 copy.14
  23.7 0.8 cosine_convert_fusion
  24.5 23.8 %convert_bitcast_fusion.2 = bf16[4,8,2,256,1024]{4,0,1,3,2:T(4,128)(2,1)} fusion(bf16[2,256,8,1024]{3,2,1,0:T(8,128)(2,1)} %bitcast.93, bf16[4,1,2]{0,2,1:T(2,128)(2,1)S(1)} %get-tuple-element.7, bf16[4,1,2]{0,2,1:T(2,128)(2,1)S(1)} %get-tuple-element.6), kind=kOutput, calls=%fused_computation.9 | convolution fusion | flops 83886144 | bytes 41943072 | tf_op jit(solution)/shard_map/tsqb,fct->fqcsb/dot_general | solution.py:39
  48.2 23.3 %copy.10 = bf16[4,8,2,256,1024]{4,3,2,1,0:T(8,128)(2,1)} copy(bf16[4,8,2,256,1024]{4,0,1,3,2:T(4,128)(2,1)} %convert_bitcast_fusion.2) | data formatting | bytes 67108864 | tf_op jit(solution)/shard_map/convert_element_type | solution.py:41
  71.6 0.0 copy-start
  71.6 7.4 all-to-all-start
  79.0 0.0 all-reduce.3.cloned.1.call-start
  79.0 0.0 copy-done
  79.1 0.6 fusion.27
  84.8 720.9 %all-to-all-done = bf16[32,2,256,1024]{3,2,1,0:T(8,128)(2,1)} async-done(((bf16[32,2,256,1024]{3,2,1,0:T(8,128)(2,1)}), bf16[32,2,256,1024]{3,2,1,0:T(8,128)(2,1)}, u32[]{:S(2)}, u32[]{:S(2)}) %all-to-all-start) | async-done | bytes 33554464 | tf_op jit(solution)/shard_map/all_to_all | solution.py:43
  805.7 32.3 %convert_bitcast_fusion.1 = f32[1,2,32,256,1024]{4,3,1,2,0:T(8,128)} fusion(bf16[32,2,256,1024]{3,2,1,0:T(8,128)(2,1)} %all-to-all-done), kind=kLoop, calls=%fused_computation.5 | loop fusion | flops 16777216 | bytes 100663296 | tf_op jit(solution)/shard_map/convert_element_type | solution.py:45
  838.0 43.7 %copy.11 = f32[1,2,32,256,1024]{4,3,2,1,0:T(8,128)} copy(f32[1,2,32,256,1024]{4,3,1,2,0:T(8,128)} %convert_bitcast_fusion.1) | data formatting | bytes 134217728 | tf_op jit(solution)/shard_map/convert_element_type | solution.py:45
  881.7 42.7 %fusion.1 = bf16[2,8192,1024]{2,1,0:T(8,128)(2,1)} fusion(f32[2,8192,1024]{2,1,0:T(8,128)} %bitcast.8, bf16[1,2,8192,1024]{3,2,1,0:T(8,128)(2,1)} %param.5), kind=kLoop, calls=%fused_computation.3 | loop fusion | flops 50331648 | bytes 134217728 | tf_op jit(solution)/shard_map/convert_element_type | solution.py:45
  924.3 12.3 dynamic-slice_select_fusion.1
  936.6 0.0 all-reduce.3.cloned.1.call-update
  937.9 43.1 %fusion.2 = bf16[1,2,8192,1024]{3,2,1,0:T(8,128)(2,1)} fusion(bf16[1,2,8192,1024]{3,2,1,0:T(8,128)(2,1)} %param.5, f32[1,2,32,256,1024]{4,3,2,1,0:T(8,128)} %copy.11), kind=kLoop, calls=%fused_computation.4 | loop fusion | flops 50331648 | bytes 134217728 | tf_op jit(solution)/shard_map/convert_element_type | solution.py:45
  981.0 492.7 %all-reduce.3.cloned.1.call-done = (bf16[2,8192,256]{2,1,0:T(8,128)(2,1)}, bf16[2,8192,256]{2,1,0:T(8,128)(2,1)}) async-done(((bf16[2,8192,256]{2,1,0:T(8,128)(2,1)}, bf16[2,8192,256]{2,1,0:T(8,128)(2,1)}), (bf16[2,8192,256]{2,1,0:T(8,128)(2,1)}, bf16[2,8192,256]{2,1,0:T(8,128)(2,1)})) %all-reduce.3.cloned.1.call-update) | async-done | bytes 16777232 | tf_op jit(solution)/shard_map/psum | solution.py:15
  1473.7 18.2 %fusion.12 = f32[1024,8192]{1,0:T(8,128)} fusion(bf16[2,8192,256]{2,1,0:T(8,128)(2,1)} %get-tuple-element.2, bf16[2,8192,1024]{2,1,0:T(8,128)(2,1)} %fusion.1, s32[]{:T(128)S(6)} %select_n.68), kind=kOutput, calls=%fused_computation.25 | convolution fusion | flops 4294967296 | bytes 38273028 | tf_op jit(solution)/shard_map/dot_general | solution.py:22
  1491.9 0.0 slice-done
  1491.9 0.0 slice-done.1
  1491.9 14.3 fusion.11
  1506.2 0.0 slice-start.2
  1506.2 0.0 slice-start.3
  1506.2 18.2 %fusion.9 = f32[1024,8192]{1,0:T(8,128)} fusion(bf16[2,8192,256]{2,1,0:T(8,128)(2,1)} %get-tuple-element.3, bf16[2,8192,1024]{2,1,0:T(8,128)(2,1)} %fusion.1, s32[]{:T(128)S(6)} %select_n.62), kind=kOutput, calls=%fused_computation.22 | convolution fusion | flops 4294967296 | bytes 38273028 | tf_op jit(solution)/shard_map/dot_general | solution.py:22
  1524.4 0.0 slice-done.2
  1524.4 0.0 slice-done.3
  1524.4 14.2 fusion.7
  1538.6 14.2 fusion.10
  1552.8 14.4 fusion.8
  1567.2 39.1 %fusion.4 = bf16[1,1,1024,8192]{3,2,1,0:T(8,128)(2,1)} fusion(f32[1024,8192]{1,0:T(8,128)} %fusion.12, f32[1024,8192]{1,0:T(8,128)} %fusion.9, f32[1024,8192]{1,0:T(8,128)} %fusion.7, bf16[2,8192,256]{2,1,0:T(8,128)(2,1)} %get-tuple-element.2, bf16[2,8192,1024]{2,1,0:T(8,128)(2,1)} %fusion.1, s32[]{:T(128)S(6)} %add.81, s32[]{:T(128)S(6)} %select_n.68), kind=kOutput, calls=%fused_computation.11 | convolution fusion | flops 4328521728 | bytes 122159112 | tf_op jit(solution)/shard_map/dot_general | solution.py:22
  1606.3 39.1 %fusion.3 = bf16[1,1,1024,8192]{3,2,1,0:T(8,128)(2,1)} fusion(f32[1024,8192]{1,0:T(8,128)} %fusion.11, f32[1024,8192]{1,0:T(8,128)} %fusion.8, f32[1024,8192]{1,0:T(8,128)} %fusion.10, bf16[2,8192,256]{2,1,0:T(8,128)(2,1)} %get-tuple-element.2, bf16[2,8192,1024]{2,1,0:T(8,128)(2,1)} %fusion.1, s32[]{:T(128)S(6)} %add.81, s32[]{:T(128)S(6)} %select_n.68), kind=kOutput, calls=%fused_computation.10 | convolution fusion | flops 4328521728 | bytes 122159112 | tf_op jit(solution)/shard_map/dot_general | solution.py:22
  1645.5 23.0 %pad_maximum_fusion = bf16[1,2,1024,8192]{3,2,1,0:T(8,128)(2,1)} fusion(bf16[1,1,1024,8192]{3,2,1,0:T(8,128)(2,1)} %fusion.4, bf16[1,1,1024,8192]{3,2,1,0:T(8,128)(2,1)} %fusion.3), kind=kLoop, calls=%fused_computation.6 | loop fusion | flops 16777216 | bytes 67108864 | tf_op jit(solution)/shard_map/stack | solution.py:59
  (5 shorter events, 0.0 us)
Async XLA Ops:
  71.6 7.5 copy-start
  71.6 734.1 %all-to-all-start = ((bf16[32,2,256,1024]{3,2,1,0:T(8,128)(2,1)}), bf16[32,2,256,1024]{3,2,1,0:T(8,128)(2,1)}, u32[]{:S(2)}, u32[]{:S(2)}) async-start(bf16[32,2,256,1024]{3,2,1,0:T(8,128)(2,1)} %bitcast.87), calls=%async_computation | async-start | bytes 67108864 | tf_op jit(solution)/shard_map/all_to_all | solution.py:43
  79.0 1394.7 %all-reduce.3.cloned.1.call-start = ((), (), s32[]{:S(2)}) async-start(), calls=%async_computation.1 | async-start | bytes 33554432 | tf_op jit(solution)/shard_map/psum | solution.py:15
  1473.7 18.2 %slice-start = ((s8[8388608]{0:T(1024)(128)(4,1)}), s8[4194304]{0:T(1024)(128)(4,1)S(1)}, s32[]{:S(2)}) async-start(s8[8388608]{0:T(1024)(128)(4,1)} %bitcast.88), calls=%async_computation.2 | async-start | bytes 8388608
  1473.7 18.2 %slice-start.1 = ((s8[8388608]{0:T(1024)(128)(4,1)}), s8[4194304]{0:T(1024)(128)(4,1)S(1)}, s32[]{:S(2)}) async-start(s8[8388608]{0:T(1024)(128)(4,1)} %bitcast.88), calls=%async_computation.3 | async-start | bytes 8388608
  1506.2 18.2 %slice-start.2 = ((s8[8388608]{0:T(1024)(128)(4,1)}), s8[4194304]{0:T(1024)(128)(4,1)S(1)}, s32[]{:S(2)}) async-start(s8[8388608]{0:T(1024)(128)(4,1)} %bitcast.90), calls=%async_computation.4 | async-start | bytes 8388608
  1506.2 18.2 %slice-start.3 = ((s8[8388608]{0:T(1024)(128)(4,1)}), s8[4194304]{0:T(1024)(128)(4,1)S(1)}, s32[]{:S(2)}) async-start(s8[8388608]{0:T(1024)(128)(4,1)} %bitcast.90), calls=%async_computation.5 | async-start | bytes 8388608
Sparse Core Ops, SparseCore 0:
  936.8 536.8 all-reduce.2
where the time goes:
time: 1680 us
  waiting for transfers between devices  1210 us (72%)
  matrix products  195 us (12%)
  other arithmetic  154 us (9%)
  local copies, waits for them, and re-layouts  84.2 us (5%)
  between operations  20.7 us (1%)
    all_to_all x1, waiting for transfers between devices, body(): lax.all_to_all(grouped, ('freq', 'row'), split_axis=0, concat_axis=2, til...  721 us
    psum x1, waiting for transfers between devices, spread(): return lax.psum(kept, axis)  493 us
    dot_general x8, matrix products, product(): lax.dot_general(first, second, dims, preferred_element_type=jnp.float32)  172 us
    convert_element_type x2, other arithmetic, body(): (prior[0].astype(jnp.float32) + arrived.astype(jnp.float32)).astype(jnp.b...  85.7 us
    convert_element_type x1, local copies, waits for them, and re-layouts, body(): arrived.astype(jnp.float32)  43.7 us
  transfers between devices with their start and end apart: 2, of which 2 were waited for; matrix products, arithmetic and copies ran while one was open for 3% of the time, Pallas kernels for 0%

commit v1 on v0

--- a/solution.py
+++ b/solution.py
@@ -40,7 +40,15 @@
         "tsqb,fct->fqcsb", blocked, twiddle, preferred_element_type=jnp.float32
     ).astype(jnp.bfloat16)
     grouped = transformed.reshape(freq_count * row_count, 2, shots_local, block_rows)
-    arrived = lax.all_to_all(grouped, ("freq", "row"), split_axis=0, concat_axis=2, tiled=True)
+    arrived = jnp.concatenate(
+        lax.all_to_all(
+            jnp.stack(jnp.split(grouped, lax.axis_size(("freq", "row")), axis=0)),
+            ("freq", "row"),
+            0,
+            0,
+        ),
+        axis=2,
+    )
     arrived = arrived.reshape(2, freq_count * row_count * shots_local, block_rows)
     spectrum = (prior[0].astype(jnp.float32) + arrived.astype(jnp.float32)).astype(jnp.bfloat16)
     panels_each = block_rows // PANEL

time: 1680 us -> 1740 us (1.036)
  local copies, waits for them, and re-layouts: 84.2 us -> 140 us
    unnamed x11 -> x44, local copies, waits for them, and re-layouts: 16.5 us -> 71.4 us
where the time goes in v1:
time: 1740 us; the launch traced here: 1730 us
  waiting for transfers between devices  1210 us (70%)
  matrix products  195 us (11%)
  other arithmetic  154 us (9%)
  local copies, waits for them, and re-layouts  140 us (8%)
  between operations  20.9 us (1%)
    all_to_all x1, waiting for transfers between devices, body(): lax.all_to_all(jnp.stack(jnp.split(grouped, lax.axis_size(('freq', 'row')...  721 us
    psum x1, waiting for transfers between devices, spread(): return lax.psum(kept, axis)  493 us
    dot_general x8, matrix products, product(): lax.dot_general(first, second, dims, preferred_element_type=jnp.float32)  171 us
    convert_element_type x2, other arithmetic, body(): (prior[0].astype(jnp.float32) + arrived.astype(jnp.float32)).astype(jnp.b...  85.7 us
    unnamed x44, local copies, waits for them, and re-layouts  71.4 us
    convert_element_type x1, local copies, waits for them, and re-layouts, body(): arrived.astype(jnp.float32)  43.7 us
  transfers between devices with their start and end apart: 2, of which 2 were waited for; matrix products, arithmetic and copies ran while one was open for 3% of the time, Pallas kernels for 0%

profile of v1, /device:TPU:0, one launch (start us, length us, event | category | flops | bytes accessed | tf_op | source)
XLA Modules:
  0.0 1731.6 jit_solution(13340839344358983628)
XLA Ops:
  7.2 16.5 copy.45
  24.5 23.8 %convert_bitcast_fusion.2 = bf16[4,8,2,256,1024]{4,0,1,3,2:T(4,128)(2,1)} fusion(bf16[2,256,8,1024]{3,2,1,0:T(8,128)(2,1)} %bitcast.249, bf16[4,1,2]{0,2,1:T(2,128)(2,1)S(1)} %get-tuple-element.7, bf16[4,1,2]{0,2,1:T(2,128)(2,1)S(1)} %get-tuple-element.6), kind=kOutput, calls=%fused_computation.9 | convolution fusion | flops 83886144 | bytes 41943072 | tf_op jit(solution)/shard_map/tsqb,fct->fqcsb/dot_general | solution.py:39
  48.3 23.3 %copy.41 = bf16[4,8,2,256,1024]{4,3,2,1,0:T(8,128)(2,1)} copy(bf16[4,8,2,256,1024]{4,0,1,3,2:T(4,128)(2,1)} %convert_bitcast_fusion.2) | data formatting | bytes 67108864 | tf_op jit(solution)/shard_map/convert_element_type | solution.py:41
  71.6 2.4 fusion.44
  74.0 3.0 fusion.43
  77.0 3.0 fusion.42
  80.1 3.0 fusion.41
  83.1 3.0 fusion.40
  86.1 2.3 fusion.39
  88.3 2.3 fusion.38
  90.6 2.3 fusion.37
  95.1 2.3 fusion.35
  97.4 2.3 fusion.34
  99.6 2.3 fusion.33
  101.9 2.3 fusion.32
  127.6 7.4 all-to-all-start
  140.8 720.9 %all-to-all-done = bf16[32,1,2,256,1024]{4,3,2,1,0:T(8,128)(2,1)} async-done(((bf16[32,1,2,256,1024]{4,3,2,1,0:T(8,128)(2,1)}), bf16[32,1,2,256,1024]{4,3,2,1,0:T(8,128)(2,1)}, u32[]{:S(2)}, u32[]{:S(2)}) %all-to-all-start) | async-done | bytes 33554464 | tf_op jit(solution)/shard_map/all_to_all | solution.py:44
  861.7 32.5 %convert_bitcast_fusion.1 = f32[1,2,32,256,1024]{4,3,1,0,2:T(8,128)} fusion(bf16[32,1,2,256,1024]{4,3,2,1,0:T(8,128)(2,1)} %all-to-all-done), kind=kLoop, calls=%fused_computation.5 | loop fusion | flops 16777216 | bytes 100663296 | tf_op jit(solution)/shard_map/convert_element_type | solution.py:53
  894.1 43.7 %copy.42 = f32[1,2,32,256,1024]{4,3,2,1,0:T(8,128)} copy(f32[1,2,32,256,1024]{4,3,1,0,2:T(8,128)} %convert_bitcast_fusion.1) | data formatting | bytes 134217728 | tf_op jit(solution)/shard_map/convert_element_type | solution.py:53
  937.9 42.7 %fusion.1 = bf16[2,8192,1024]{2,1,0:T(8,128)(2,1)} fusion(f32[2,8192,1024]{2,1,0:T(8,128)} %bitcast.39, bf16[1,2,8192,1024]{3,2,1,0:T(8,128)(2,1)} %param.5), kind=kLoop, calls=%fused_computation.3 | loop fusion | flops 50331648 | bytes 134217728 | tf_op jit(solution)/shard_map/convert_element_type | solution.py:53
  980.5 12.3 dynamic-slice_select_fusion.1
  994.1 43.1 %fusion.2 = bf16[1,2,8192,1024]{3,2,1,0:T(8,128)(2,1)} fusion(bf16[1,2,8192,1024]{3,2,1,0:T(8,128)(2,1)} %param.5, f32[1,2,32,256,1024]{4,3,2,1,0:T(8,128)} %copy.42), kind=kLoop, calls=%fused_computation.4 | loop fusion | flops 50331648 | bytes 134217728 | tf_op jit(solution)/shard_map/convert_element_type | solution.py:53
  1037.2 492.7 %all-reduce.3.cloned.1.call-done = (bf16[2,8192,256]{2,1,0:T(8,128)(2,1)}, bf16[2,8192,256]{2,1,0:T(8,128)(2,1)}) async-done(((bf16[2,8192,256]{2,1,0:T(8,128)(2,1)}, bf16[2,8192,256]{2,1,0:T(8,128)(2,1)}), (bf16[2,8192,256]{2,1,0:T(8,128)(2,1)}, bf16[2,8192,256]{2,1,0:T(8,128)(2,1)})) %all-reduce.3.cloned.1.call-update) | async-done | bytes 16777232 | tf_op jit(solution)/shard_map/psum | solution.py:15
  1529.9 18.2 %fusion.12 = f32[1024,8192]{1,0:T(8,128)} fusion(bf16[2,8192,256]{2,1,0:T(8,128)(2,1)} %get-tuple-element.2, bf16[2,8192,1024]{2,1,0:T(8,128)(2,1)} %fusion.1, s32[]{:T(128)S(6)} %select_n.68), kind=kOutput, calls=%fused_computation.25 | convolution fusion | flops 4294967296 | bytes 38273028 | tf_op jit(solution)/shard_map/dot_general | solution.py:22
  1548.1 14.4 fusion.11
  1562.4 18.2 %fusion.9 = f32[1024,8192]{1,0:T(8,128)} fusion(bf16[2,8192,256]{2,1,0:T(8,128)(2,1)} %get-tuple-element.3, bf16[2,8192,1024]{2,1,0:T(8,128)(2,1)} %fusion.1, s32[]{:T(128)S(6)} %select_n.62), kind=kOutput, calls=%fused_computation.22 | convolution fusion | flops 4294967296 | bytes 38273028 | tf_op jit(solution)/shard_map/dot_general | solution.py:22
  1580.6 14.2 fusion.7
  1594.8 14.2 fusion.10
  1608.9 14.4 fusion.8
  1623.3 39.0 %fusion.4 = bf16[1,1,1024,8192]{3,2,1,0:T(8,128)(2,1)} fusion(f32[1024,8192]{1,0:T(8,128)} %fusion.12, f32[1024,8192]{1,0:T(8,128)} %fusion.9, f32[1024,8192]{1,0:T(8,128)} %fusion.7, bf16[2,8192,256]{2,1,0:T(8,128)(2,1)} %get-tuple-element.2, bf16[2,8192,1024]{2,1,0:T(8,128)(2,1)} %fusion.1, s32[]{:T(128)S(6)} %add.81, s32[]{:T(128)S(6)} %select_n.68), kind=kOutput, calls=%fused_computation.11 | convolution fusion | flops 4328521728 | bytes 122159112 | tf_op jit(solution)/shard_map/dot_general | solution.py:22
  1662.4 39.0 %fusion.3 = bf16[1,1,1024,8192]{3,2,1,0:T(8,128)(2,1)} fusion(f32[1024,8192]{1,0:T(8,128)} %fusion.11, f32[1024,8192]{1,0:T(8,128)} %fusion.8, f32[1024,8192]{1,0:T(8,128)} %fusion.10, bf16[2,8192,256]{2,1,0:T(8,128)(2,1)} %get-tuple-element.2, bf16[2,8192,1024]{2,1,0:T(8,128)(2,1)} %fusion.1, s32[]{:T(128)S(6)} %add.81, s32[]{:T(128)S(6)} %select_n.68), kind=kOutput, calls=%fused_computation.10 | convolution fusion | flops 4328521728 | bytes 122159112 | tf_op jit(solution)/shard_map/dot_general | solution.py:22
  1701.4 23.0 %pad_maximum_fusion = bf16[1,2,1024,8192]{3,2,1,0:T(8,128)(2,1)} fusion(bf16[1,1,1024,8192]{3,2,1,0:T(8,128)(2,1)} %fusion.4, bf16[1,1,1024,8192]{3,2,1,0:T(8,128)(2,1)} %fusion.3), kind=kLoop, calls=%fused_computation.6 | loop fusion | flops 16777216 | bytes 67108864 | tf_op jit(solution)/shard_map/stack | solution.py:67
  (39 shorter events, 27.2 us)
Async XLA Ops:
  71.6 39.3 %copy-start = (bf16[4,8,2,256,1024]{4,3,2,1,0:T(8,128)(2,1)S(1)}, bf16[4,8,2,256,1024]{4,3,2,1,0:T(8,128)(2,1)}, u32[]{:S(2)}) copy-start(bf16[4,8,2,256,1024]{4,3,2,1,0:T(8,128)(2,1)} %copy.41) | copy-start | bytes 100663296
  127.6 7.5 copy-start.1
  127.6 734.1 %all-to-all-start = ((bf16[32,1,2,256,1024]{4,3,2,1,0:T(8,128)(2,1)}), bf16[32,1,2,256,1024]{4,3,2,1,0:T(8,128)(2,1)}, u32[]{:S(2)}, u32[]{:S(2)}) async-start(bf16[32,1,2,256,1024]{4,3,2,1,0:T(8,128)(2,1)} %fusion.13), calls=%async_computation | async-start | bytes 67108864 | tf_op jit(solution)/shard_map/all_to_all | solution.py:44
  135.0 1394.9 %all-reduce.3.cloned.1.call-start = ((), (), s32[]{:S(2)}) async-start(), calls=%async_computation.1 | async-start | bytes 33554432 | tf_op jit(solution)/shard_map/psum | solution.py:15
  1529.9 18.2 %slice-start = ((s8[8388608]{0:T(1024)(128)(4,1)}), s8[4194304]{0:T(1024)(128)(4,1)S(1)}, s32[]{:S(2)}) async-start(s8[8388608]{0:T(1024)(128)(4,1)} %bitcast.244), calls=%async_computation.2 | async-start | bytes 8388608
  1529.9 18.2 %slice-start.1 = ((s8[8388608]{0:T(1024)(128)(4,1)}), s8[4194304]{0:T(1024)(128)(4,1)S(1)}, s32[]{:S(2)}) async-start(s8[8388608]{0:T(1024)(128)(4,1)} %bitcast.244), calls=%async_computation.3 | async-start | bytes 8388608
  1562.4 18.2 %slice-start.2 = ((s8[8388608]{0:T(1024)(128)(4,1)}), s8[4194304]{0:T(1024)(128)(4,1)S(1)}, s32[]{:S(2)}) async-start(s8[8388608]{0:T(1024)(128)(4,1)} %bitcast.246), calls=%async_computation.4 | async-start | bytes 8388608
  1562.4 18.2 %slice-start.3 = ((s8[8388608]{0:T(1024)(128)(4,1)}), s8[4194304]{0:T(1024)(128)(4,1)S(1)}, s32[]{:S(2)}) async-start(s8[8388608]{0:T(1024)(128)(4,1)} %bitcast.246), calls=%async_computation.5 | async-start | bytes 8388608
Sparse Core Ops, SparseCore 0:
  993.0 536.8 all-reduce.2
